TPU v7x, 32 devices: a whole 2x2x4 slice. The times are simulated.
32 devices in a mesh: groups: 2 (over x), chan: 16 (over z, y, core).
Axes of the slice: x: 2, y: 2, z: 4, core: 2. Of those that a mesh axis runs over, the one named last changes fastest.
Arguments:
- sky_data: bfloat16 [1024, 512, 2, 256], P('groups', 'chan'), parts along dimension 0, may hold values from -1.1953125 to 1.1953125
- beam_gains: bfloat16 [1024, 512, 256], P('groups', 'chan'), parts along dimension 0, may hold values from 0.099609375 to 1
- mixing: float32 [1024, 4], P(('groups', 'chan')), parts along dimension 0, may hold values from -0.25 to 0.25
- noise_levels: int32 [512], P('chan'), may hold values from 1 to 16
- threshold_levels: int32 [4, 2], replicated, may hold values from 1 to 8
- start_sources: float32 [1024, 4, 256], P(('groups', 'chan')), parts along dimension 0, may hold values from -6 to 6
Outputs:
- sources: float32 [1024, 4, 256], P(('groups', 'chan')), parts along dimension 0
There are 2 independent parts, one for each index of `groups`. A program takes and returns all parts, laid end to end along the dimension named above; an argument that names none is the same for every part. Nothing has to cross between parts.
All inputs are finite; a program needn't handle non-finite values.
Results may differ from a plain program's by a relative error of at most 0.025.
Values may be sent and summed in bfloat16 or wider, within the bound.
No kernel may reach another device: no remote copies, remote signals or barrier semaphores. Data moves between devices by JAX's collectives and lax.ppermute only.
A program may use at most 128 MiB of HBM per device.

v0:
```python
import math

import jax
import jax.numpy as jnp
from jax import lax
from jax.sharding import PartitionSpec as P

ITERS = 2


def padded_2(cells, sides, width):
    for axis, dim in sides:
        count = lax.axis_size(axis)
        ends = count - 1
        head = lax.slice_in_dim(cells, 0, width, axis=dim)
        tail = lax.slice_in_dim(cells, cells.shape[dim] - width, cells.shape[dim], axis=dim)
        cells = jnp.concatenate(
            [
                lax.ppermute(tail, axis, [(i, (i + 1) % count) for i in range(ends)]),
                cells,
                lax.ppermute(head, axis, [((i + 1) % count, i) for i in range(ends)]),
            ],
            axis=dim,
        )
    return cells


def dft_tables(length):
    positions = jnp.arange(length, dtype=jnp.int32)
    angles = (positions[:, None] * positions[None, :] % length).astype(jnp.float32) * (
        2.0 * math.pi / length
    )
    norm_factor = 1.0 / math.sqrt(length)
    return (
        (jnp.cos(angles) * norm_factor).astype(jnp.bfloat16),
        (-jnp.sin(angles) * norm_factor).astype(jnp.bfloat16),
    )


def column_part(rounded, col_cat):
    row_count, source_count, col_count = rounded.shape
    product = jnp.dot(
        rounded.reshape(row_count * source_count, col_count),
        col_cat,
        preferred_element_type=jnp.float32,
    )
    return product.astype(jnp.bfloat16).reshape(row_count, source_count * 2 * col_count)


def combine_forward(real_prod, imag_prod, source_count, col_count):
    real_prod = real_prod.reshape(real_prod.shape[0], source_count, 2, col_count)
    imag_prod = imag_prod.reshape(imag_prod.shape[0], source_count, 2, col_count)
    real_out = real_prod[:, :, 0] - imag_prod[:, :, 1]
    imag_out = real_prod[:, :, 1] + imag_prod[:, :, 0]
    return jnp.stack([real_out, imag_out], axis=2)


def inverse_rows(row_real, row_imag, packed_grad, col_back, source_count, col_count):
    real_prod = jnp.dot(row_real, packed_grad, preferred_element_type=jnp.float32)
    imag_prod = jnp.dot(row_imag, packed_grad, preferred_element_type=jnp.float32)
    real_prod = real_prod.reshape(real_prod.shape[0], source_count, 2, col_count)
    imag_prod = imag_prod.reshape(imag_prod.shape[0], source_count, 2, col_count)
    real_out = real_prod[:, :, 0] + imag_prod[:, :, 1]
    imag_out = real_prod[:, :, 1] - imag_prod[:, :, 0]
    joined = jnp.concatenate([real_out, imag_out], axis=-1).astype(jnp.bfloat16)
    result = jnp.dot(
        joined.reshape(-1, 2 * col_count), col_back, preferred_element_type=jnp.float32
    )
    return result.reshape(real_prod.shape[0], source_count, col_count)


def block_gradient(fourier, data_block, beam_block, mix_block, level_block):
    predicted = jnp.einsum("ct,ktzl->kczl", mix_block, fourier)
    beam_gain = beam_block.astype(jnp.float32)[:, :, None, :]
    residual = data_block.astype(jnp.float32) - beam_gain * predicted
    weight = level_block.astype(jnp.float32) * 0.25
    weighted = weight[None, :, None, None] * beam_gain * residual
    summed = jnp.einsum("cs,kczl->kszl", mix_block, weighted)
    return summed.astype(jnp.bfloat16)


def smooth_rows(padded, spacing, row_count):
    return (
        padded[0:row_count]
        + 2.0 * padded[spacing : spacing + row_count]
        + padded[2 * spacing : 2 * spacing + row_count]
    ) * 0.25


def smooth_cols(values, spacing):
    padded = jnp.pad(values, ((0, 0), (0, 0), (spacing, spacing)))
    return (
        padded[..., : -2 * spacing]
        + 2.0 * padded[..., spacing:-spacing]
        + padded[..., 2 * spacing :]
    ) * 0.25


def shrink(values, bound_value):
    return values - jnp.clip(values, -bound_value, bound_value)


def combine_scales(updated, smooth_one, coarse, fine_bound, coarse_bound):
    return (
        coarse
        + shrink(smooth_one - coarse, coarse_bound)
        + shrink(updated - smooth_one, fine_bound)
    )


def body(sky_data, beam_gains, mixing, noise_levels, threshold_levels, start_sources):
    strip_rows, source_count, col_count = start_sources.shape
    full_rows = strip_rows * lax.axis_size("chan")
    row_real, row_imag = dft_tables(full_rows)
    col_real, col_imag = dft_tables(col_count)
    col_cat = jnp.concatenate([col_real, col_imag], axis=1)
    col_back = jnp.concatenate([col_real, col_imag], axis=0)
    bounds = threshold_levels.astype(jnp.float32) * 0.05
    fine_bound = bounds[:, 0][:, None]
    coarse_bound = bounds[:, 1][:, None]
    sources = start_sources
    for iteration in range(ITERS):
        rounded = sources.astype(jnp.bfloat16)
        gathered = lax.all_gather(rounded, "chan", axis=0, tiled=True)
        packed = column_part(gathered, col_cat)
        fourier = combine_forward(
            jnp.dot(row_real, packed, preferred_element_type=jnp.float32),
            jnp.dot(row_imag, packed, preferred_element_type=jnp.float32),
            source_count,
            col_count,
        )
        grad_local = block_gradient(fourier, sky_data, beam_gains, mixing, noise_levels)
        packed_grad = grad_local.reshape(full_rows, source_count * 2 * col_count)
        gradient = lax.psum_scatter(
            inverse_rows(row_real, row_imag, packed_grad, col_back, source_count, col_count),
            "chan",
            scatter_dimension=0,
            tiled=True,
        )
        updated = sources + gradient
        fine_pad = padded_2(updated, (("chan", 0),), 1)
        smooth_one = smooth_cols(smooth_rows(fine_pad, 1, strip_rows), 1)
        coarse_pad = padded_2(smooth_one, (("chan", 0),), 2)
        coarse = smooth_cols(smooth_rows(coarse_pad, 2, strip_rows), 2)
        sources = combine_scales(updated, smooth_one, coarse, fine_bound, coarse_bound)
    return sources


def solution(mesh):
    return jax.shard_map(
        body,
        mesh=mesh,
        in_specs=(
            P("groups", "chan", None, None),
            P("groups", "chan", None),
            P(("groups", "chan"), None),
            P("chan"),
            P(),
            P(("groups", "chan"), None, None),
        ),
        out_specs=P(("groups", "chan"), None, None),
        check_vma=False,
    )
```

profile of v0, /device:TPU:1, one launch (start us, length us, event | category | flops | bytes accessed | tf_op | source)
XLA Modules:
  0.0 385.0 jit_solution(10828506220403828621)
XLA Ops:
  8.2 11.3 %convert_element_type.111 = f32[512,32,256]{2,1,0:T(8,128)} convert(bf16[512,32,256]{2,1,0:T(8,128)(2,1)} %param.7) | non-fusion elementwise | flops 4194304 | bytes 25165824 | tf_op jit(solution)/shard_map/convert_element_type | solution.py:74
  20.6 11.7 %broadcast_multiply_fusion = f32[512,32,256]{2,1,0:T(8,128)} fusion(f32[32]{0:T(128)S(1)} %convert_multiply_fusion.1, bf16[512,32,256]{2,1,0:T(8,128)(2,1)} %param.7), kind=kLoop, calls=%fused_computation.16 | loop fusion | flops 8388608 | bytes 25165952 | tf_op jit(solution)/shard_map/mul | solution.py:77
  32.3 17.7 %all-gather.3.cloned.1.call-done = bf16[512,4,256]{2,1,0:T(4,128)(2,1)} async-done(((bf16[32,4,256]{2,1,0:T(4,128)(2,1)}), bf16[512,4,256]{2,1,0:T(4,128)(2,1)}) %all-gather.3.cloned.1.call-update) | async-done | bytes 1048592 | tf_op jit(solution)/shard_map/all_gather | solution.py:124
  54.7 3.1 reshape.71
  60.5 6.6 %fusion.67 = f32[512,4,2,256]{3,0,2,1:T(8,128)S(1)} fusion(bf16[4,2,256,512]{3,2,1,0:T(8,128)(2,1)} %bitcast.123), kind=kOutput, calls=%fused_computation.76 | convolution fusion | flops 1078198272 | bytes 6291456 | tf_op jit(solution)/shard_map/dot_general | solution.py:128
  67.2 4.9 %fusion.73 = f32[512,4,2,256]{3,0,2,1:T(8,128)S(1)} fusion(bf16[4,2,256,512]{3,2,1,0:T(8,128)(2,1)S(1)} %bitcast.124), kind=kOutput, calls=%fused_computation.78 | convolution fusion | flops 1077936128 | bytes 6291456 | tf_op jit(solution)/shard_map/dot_general | solution.py:127
  73.7 24.1 %convert_bitcast_fusion.1 = bf16[512,4,2,256]{3,1,2,0:T(4,128)(2,1)} fusion(f32[512,32,256]{2,1,0:T(8,128)} %convert_element_type.111, f32[512,32,256]{2,1,0:T(8,128)} %broadcast_multiply_fusion, bf16[512,32,2,256]{3,2,1,0:T(2,128)(2,1)} %param.6, bf16[512,4,2,256]{3,0,2,1:T(8,128)(2,1)S(1)} %pad_maximum_fusion, f32[32,4]{0,1:T(4,128)S(1)} %copy-done.2), kind=kOutput, calls=%fused_computation.57 | convolution fusion | flops 176160896 | bytes 54526464 | tf_op jit(solution)/shard_map/cs,kczl->kszl/dot_general | solution.py:78
  97.8 3.0 copy.40
  100.7 7.3 %fusion.39 = f32[512,4,2,256]{0,3,2,1:T(8,128)S(1)} fusion(bf16[512,4,2,256]{0,3,2,1:T(8,128)(2,1)S(1)} %copy.40), kind=kOutput, calls=%fused_computation.52 | convolution fusion | flops 1078198272 | bytes 6291456 | tf_op jit(solution)/shard_map/dot_general | solution.py:60
  108.1 7.3 %fusion.41 = f32[512,4,2,256]{0,3,2,1:T(8,128)S(1)} fusion(bf16[512,4,2,256]{0,3,2,1:T(8,128)(2,1)S(1)} %copy.40), kind=kOutput, calls=%fused_computation.54 | convolution fusion | flops 1077936128 | bytes 6291456 | tf_op jit(solution)/shard_map/dot_general | solution.py:59
  118.7 58.6 %reduce-scatter.3.cloned.1.call-done = f32[32,4,256]{2,0,1:T(8,128)} async-done(((f32[512,4,256]{2,0,1:T(8,128)}), f32[32,4,256]{2,0,1:T(8,128)}) %reduce-scatter.3.cloned.1.call-update) | async-done | bytes 131088 | tf_op jit(solution)/shard_map/reduce_scatter | solution.py:134
  178.3 4.9 %collective-permute-start = (f32[1,4,256]{2,0,1:T(1,128)S(1)}, f32[1,4,256]{2,0,1:T(1,128)S(1)}, u32[]{:S(2)}, u32[]{:S(2)}) collective-permute-start(f32[1,4,256]{2,0,1:T(1,128)S(1)} %get-tuple-element.21), channel_id=1, source_target_pairs={{0,1},{1,2},{2,3},{3,4},{4,5},{5,6},{6,7},{7,8},{8,9},{9,10},{10,1... | collective-permute-start | bytes 12296 | tf_op jit(solution)/shard_map/ppermute | solution.py:19
  192.6 3.5 collective-permute-done.3
  197.1 38.0 %all-gather.5.cloned.1.call-done = bf16[512,4,256]{2,0,1:T(8,128)(2,1)} async-done(((bf16[32,4,256]{2,0,1:T(8,128)(2,1)}), bf16[512,4,256]{2,0,1:T(8,128)(2,1)}) %all-gather.5.cloned.1.call-update) | async-done | bytes 1048592 | tf_op jit(solution)/shard_map/all_gather | solution.py:124
  243.7 4.9 %fusion.64 = f32[512,4,2,256]{3,0,2,1:T(8,128)S(1)} fusion(bf16[4,2,256,512]{3,2,1,0:T(8,128)(2,1)S(1)} %bitcast.125), kind=kOutput, calls=%fused_computation.75 | convolution fusion | flops 1078198272 | bytes 6291456 | tf_op jit(solution)/shard_map/dot_general | solution.py:128
  248.6 4.9 %fusion.70 = f32[512,4,2,256]{3,0,2,1:T(8,128)S(1)} fusion(bf16[4,2,256,512]{3,2,1,0:T(8,128)(2,1)S(1)} %bitcast.126), kind=kOutput, calls=%fused_computation.77 | convolution fusion | flops 1077936128 | bytes 6291456 | tf_op jit(solution)/shard_map/dot_general | solution.py:127
  254.6 23.9 %convert_bitcast_fusion = bf16[512,4,2,256]{3,1,2,0:T(4,128)(2,1)} fusion(f32[512,32,256]{2,1,0:T(8,128)} %convert_element_type.111, f32[512,32,256]{2,1,0:T(8,128)} %broadcast_multiply_fusion, bf16[512,32,2,256]{3,2,1,0:T(2,128)(2,1)} %param.6, bf16[512,4,2,256]{3,0,2,1:T(8,128)(2,1)S(1)} %pad_maximum_fusion.1, f32[32,4]{0,1:T(4,128)S(1)} %copy-done.2), kind=kOutput, calls=%fused_computation.56 | convolution fusion | flops 176160896 | bytes 54526464 | tf_op jit(solution)/shard_map/cs,kczl->kszl/dot_general | solution.py:78
  278.6 3.0 copy.48
  281.5 7.3 %fusion.35 = f32[512,4,2,256]{0,3,2,1:T(8,128)S(1)} fusion(bf16[512,4,2,256]{0,3,2,1:T(8,128)(2,1)S(1)} %copy.48), kind=kOutput, calls=%fused_computation.48 | convolution fusion | flops 1078198272 | bytes 6291456 | tf_op jit(solution)/shard_map/dot_general | solution.py:60
  288.9 7.5 %fusion.37 = f32[512,4,2,256]{0,3,2,1:T(8,128)S(1)} fusion(bf16[512,4,2,256]{0,3,2,1:T(8,128)(2,1)S(1)} %copy.48), kind=kOutput, calls=%fused_computation.50 | convolution fusion | flops 1077936128 | bytes 6291456 | tf_op jit(solution)/shard_map/dot_general | solution.py:59
  299.8 58.6 %reduce-scatter.5.cloned.1.call-done = f32[32,4,256]{2,0,1:T(8,128)} async-done(((f32[512,4,256]{2,0,1:T(8,128)}), f32[32,4,256]{2,0,1:T(8,128)}) %reduce-scatter.5.cloned.1.call-update) | async-done | bytes 131088 | tf_op jit(solution)/shard_map/reduce_scatter | solution.py:134
  359.4 4.9 %collective-permute-start.4 = (f32[1,4,256]{2,0,1:T(1,128)S(1)}, f32[1,4,256]{2,0,1:T(1,128)S(1)}, u32[]{:S(2)}, u32[]{:S(2)}) collective-permute-start(f32[1,4,256]{2,0,1:T(1,128)S(1)} %get-tuple-element.17), channel_id=1, source_target_pairs={{0,1},{1,2},{2,3},{3,4},{4,5},{5,6},{6,7},{7,8},{8,9},{9,10},{10,1... | collective-permute-start | bytes 12296 | tf_op jit(solution)/shard_map/ppermute | solution.py:19
  366.2 3.0 collective-permute-done.5
  373.7 3.5 collective-permute-done.7
  (72 shorter events, 47.7 us)
Async XLA Ops:
  6.5 43.5 %all-gather.3.cloned.1.call-start = ((), (), s32[]{:S(2)}) async-start(), calls=%async_computation.2 | async-start | bytes 1114112 | tf_op jit(solution)/shard_map/all_gather | solution.py:124
  8.1 12.5 %copy-start.6 = (s32[32]{0:T(128)S(1)}, s32[32]{0:T(128)}, u32[]{:S(2)}) copy-start(s32[32]{0:T(128)} %param.9) | copy-start | bytes 388
  8.1 169.2 %reduce-scatter.3.cloned.1.call-start = ((), (), s32[]{:S(2)}) async-start(), calls=%async_computation.3 | async-start | bytes 2228224 | tf_op jit(solution)/shard_map/reduce_scatter | solution.py:134
  60.5 6.7 %copy-start = (bf16[2048,512]{1,0:T(8,128)(2,1)S(1)}, bf16[2048,512]{1,0:T(8,128)(2,1)}, u32[]{:S(2)}) copy-start(bf16[2048,512]{1,0:T(8,128)(2,1)} %copy.58) | copy-start | bytes 6291460
  73.0 0.7 copy-start.2
  118.6 58.7 %copy-start.1 = (f32[32,4,256]{2,1,0:T(4,128)S(1)}, f32[32,4,256]{2,1,0:T(4,128)}, u32[]{:S(2)}) copy-start(f32[32,4,256]{2,1,0:T(4,128)} %param.11) | copy-start | bytes 393220
  118.6 66.4 %copy-start.5 = (s32[4,2]{0,1:T(2,128)S(1)}, s32[4,2]{0,1:T(2,128)}, u32[]{:S(2)}) copy-start(s32[4,2]{0,1:T(2,128)} %param.10) | copy-start | bytes 100
  118.7 116.4 %all-gather.5.cloned.1.call-start = ((), (), s32[]{:S(2)}) async-start(), calls=%async_computation.4 | async-start | bytes 1114112 | tf_op jit(solution)/shard_map/all_gather | solution.py:124
  178.3 6.8 %collective-permute-start = (f32[1,4,256]{2,0,1:T(1,128)S(1)}, f32[1,4,256]{2,0,1:T(1,128)S(1)}, u32[]{:S(2)}, u32[]{:S(2)}) collective-permute-start(f32[1,4,256]{2,0,1:T(1,128)S(1)} %get-tuple-element.21), channel_id=1, source_target_pairs={{0,1},{1,2},{2,3},{3,4},{4,5},{5,6},{6,7},{7,8},{8,9},{9,10},{10,1... | collective-permute-start | bytes 12296 | tf_op jit(solution)/shard_map/ppermute | solution.py:19
  183.1 4.9 %collective-permute-start.1 = (f32[1,4,256]{2,0,1:T(1,128)S(1)}, f32[1,4,256]{2,0,1:T(1,128)S(1)}, u32[]{:S(2)}, u32[]{:S(2)}) collective-permute-start(f32[1,4,256]{2,0,1:T(1,128)S(1)} %get-tuple-element.22), channel_id=1, source_target_pairs={{1,0},{2,1},{3,2},{4,3},{5,4},{6,5},{7,6},{8,7},{9,8},{10,9},{11,1... | collective-permute-start | bytes 12296 | tf_op jit(solution)/shard_map/ppermute | solution.py:21
  188.3 4.4 %collective-permute-start.2 = (f32[2,4,256]{2,0,1:T(2,128)S(1)}, f32[2,4,256]{2,0,1:T(2,128)S(1)}, u32[]{:S(2)}, u32[]{:S(2)}) collective-permute-start(f32[2,4,256]{2,0,1:T(2,128)S(1)} %get-tuple-element.19), channel_id=1, source_target_pairs={{0,1},{1,2},{2,3},{3,4},{4,5},{5,6},{6,7},{7,8},{8,9},{9,10},{10,1... | collective-permute-start | bytes 24584 | tf_op jit(solution)/shard_map/ppermute | solution.py:19
  190.2 5.9 %collective-permute-start.3 = (f32[2,4,256]{2,0,1:T(2,128)S(1)}, f32[2,4,256]{2,0,1:T(2,128)S(1)}, u32[]{:S(2)}, u32[]{:S(2)}) collective-permute-start(f32[2,4,256]{2,0,1:T(2,128)S(1)} %get-tuple-element.20), channel_id=1, source_target_pairs={{1,0},{2,1},{3,2},{4,3},{5,4},{6,5},{7,6},{8,7},{9,8},{10,9},{11,1... | collective-permute-start | bytes 24584 | tf_op jit(solution)/shard_map/ppermute | solution.py:21
  192.6 4.3 %copy-start.3 = (f32[4]{0:T(128)}, f32[4]{0:T(128)S(1)}, u32[]{:S(2)}) copy-start(f32[4]{0:T(128)S(1)} %get-tuple-element.26) | copy-start | bytes 52
  197.0 161.4 %reduce-scatter.5.cloned.1.call-start = ((), (), s32[]{:S(2)}) async-start(), calls=%async_computation.5 | async-start | bytes 2228224 | tf_op jit(solution)/shard_map/reduce_scatter | solution.py:134
  299.7 77.5 %copy-start.4 = (f32[4]{0:T(128)S(1)}, f32[4]{0:T(128)}, u32[]{:S(2)}) copy-start(f32[4]{0:T(128)} %copy-done.3) | copy-start | bytes 52
  359.4 6.8 %collective-permute-start.4 = (f32[1,4,256]{2,0,1:T(1,128)S(1)}, f32[1,4,256]{2,0,1:T(1,128)S(1)}, u32[]{:S(2)}, u32[]{:S(2)}) collective-permute-start(f32[1,4,256]{2,0,1:T(1,128)S(1)} %get-tuple-element.17), channel_id=1, source_target_pairs={{0,1},{1,2},{2,3},{3,4},{4,5},{5,6},{6,7},{7,8},{8,9},{9,10},{10,1... | collective-permute-start | bytes 12296 | tf_op jit(solution)/shard_map/ppermute | solution.py:19
  364.2 4.9 %collective-permute-start.5 = (f32[1,4,256]{2,0,1:T(1,128)S(1)}, f32[1,4,256]{2,0,1:T(1,128)S(1)}, u32[]{:S(2)}, u32[]{:S(2)}) collective-permute-start(f32[1,4,256]{2,0,1:T(1,128)S(1)} %get-tuple-element.18), channel_id=1, source_target_pairs={{1,0},{2,1},{3,2},{4,3},{5,4},{6,5},{7,6},{8,7},{9,8},{10,9},{11,1... | collective-permute-start | bytes 12296 | tf_op jit(solution)/shard_map/ppermute | solution.py:21
  369.4 4.3 %collective-permute-start.6 = (f32[2,4,256]{2,0,1:T(2,128)S(1)}, f32[2,4,256]{2,0,1:T(2,128)S(1)}, u32[]{:S(2)}, u32[]{:S(2)}) collective-permute-start(f32[2,4,256]{2,0,1:T(2,128)S(1)} %get-tuple-element.15), channel_id=1, source_target_pairs={{0,1},{1,2},{2,3},{3,4},{4,5},{5,6},{6,7},{7,8},{8,9},{9,10},{10,1... | collective-permute-start | bytes 24584 | tf_op jit(solution)/shard_map/ppermute | solution.py:19
  371.3 5.9 %collective-permute-start.7 = (f32[2,4,256]{2,0,1:T(2,128)S(1)}, f32[2,4,256]{2,0,1:T(2,128)S(1)}, u32[]{:S(2)}, u32[]{:S(2)}) collective-permute-start(f32[2,4,256]{2,0,1:T(2,128)S(1)} %get-tuple-element.16), channel_id=1, source_target_pairs={{1,0},{2,1},{3,2},{4,3},{5,4},{6,5},{7,6},{8,7},{9,8},{10,9},{11,1... | collective-permute-start | bytes 24584 | tf_op jit(solution)/shard_map/ppermute | solution.py:21
Sparse Core Ops, SparseCore 0:
  9.5 40.4 all-gather.2
  118.8 58.4 reduce-scatter.2
  197.1 37.8 all-gather.4
  299.9 58.4 reduce-scatter.4
where the time goes:
time: 391 us; the launch traced here: 385 us
  waiting for transfers between devices  186 us (48%)
  matrix products  104 us (27%)
  other arithmetic  33.6 us (9%)
  local copies, waits for them, and re-layouts  24.9 us (6%)
  starting transfers between devices  22.4 us (6%)
  between operations  13.8 us (4%)
    reduce_scatter x2, waiting for transfers between devices, body(): lax.psum_scatter(inverse_rows(row_real, row_imag, packed_grad, col_back,...  117 us
    all_gather x2, waiting for transfers between devices, body(): gathered = lax.all_gather(rounded, 'chan', axis=0, tiled=True)  55.7 us
    dot_general x2, matrix products, block_gradient(): summed = jnp.einsum('cs,kczl->kszl', mix_block, weighted)  48.1 us
    dot_general x2, matrix products, inverse_rows(): jnp.dot(row_real, packed_grad, preferred_element_type=jnp.float32)  14.8 us
    dot_general x2, matrix products, inverse_rows(): jnp.dot(row_imag, packed_grad, preferred_element_type=jnp.float32)  14.7 us
    ppermute x4, starting transfers between devices, padded_2(): lax.ppermute(tail, axis, [(i, (i + 1) % count) for i in range(ends)])  13.6 us
    ppermute x4, waiting for transfers between devices, padded_2(): lax.ppermute(head, axis, [((i + 1) % count, i) for i in range(ends)])  12.9 us
    mul x1, other arithmetic, block_gradient(): weighted = weight[None, :, None, None] * beam_gain * residual  11.7 us
  transfers between devices with their start and end apart: 12, of which 8 were waited for; matrix products, arithmetic and copies ran while one was open for 6% of the time, Pallas kernels for 0%

commit v1 on v0

--- a/solution.py
+++ b/solution.py
@@ -23,6 +23,20 @@
             axis=dim,
         )
     return cells
+
+
+def gather_rows(strip, axis):
+    count = lax.axis_size(axis)
+    copies = jnp.broadcast_to(strip[None], (count,) + strip.shape)
+    joined = lax.all_to_all(copies, axis, 0, 0, tiled=True)
+    return joined.reshape((count * strip.shape[0],) + strip.shape[1:])
+
+
+def sum_rows(values, axis):
+    count = lax.axis_size(axis)
+    chunks = values.reshape((count, values.shape[0] // count) + values.shape[1:])
+    received = lax.all_to_all(chunks, axis, 0, 0, tiled=True)
+    return received.sum(axis=0)
 
 
 def dft_tables(length):
@@ -121,7 +135,7 @@
     sources = start_sources
     for iteration in range(ITERS):
         rounded = sources.astype(jnp.bfloat16)
-        gathered = lax.all_gather(rounded, "chan", axis=0, tiled=True)
+        gathered = gather_rows(rounded, "chan")
         packed = column_part(gathered, col_cat)
         fourier = combine_forward(
             jnp.dot(row_real, packed, preferred_element_type=jnp.float32),
@@ -131,11 +145,9 @@
         )
         grad_local = block_gradient(fourier, sky_data, beam_gains, mixing, noise_levels)
         packed_grad = grad_local.reshape(full_rows, source_count * 2 * col_count)
-        gradient = lax.psum_scatter(
+        gradient = sum_rows(
             inverse_rows(row_real, row_imag, packed_grad, col_back, source_count, col_count),
             "chan",
-            scatter_dimension=0,
-            tiled=True,
         )
         updated = sources + gradient
         fine_pad = padded_2(updated, (("chan", 0),), 1)

time: 391 us -> 329 us (0.84)
  the two profiles are of different devices: /device:TPU:1 before, /device:TPU:13 now
where the time goes in v1:
time: 329 us; the launch traced here: 322 us
  blocking collectives  133 us (40%)
  matrix products  91.4 us (28%)
  other arithmetic  30.4 us (9%)
  starting transfers between devices  26.3 us (8%)
  local copies, waits for them, and re-layouts  24.7 us (8%)
  waiting for transfers between devices  15.4 us (5%)
    all_to_all x2, blocking collectives, sum_rows(): received = lax.all_to_all(chunks, axis, 0, 0, tiled=True)  104 us
    dot_general x2, matrix products, block_gradient(): summed = jnp.einsum('cs,kczl->kszl', mix_block, weighted)  47.7 us
    all_to_all x1, blocking collectives, gather_rows(): joined = lax.all_to_all(copies, axis, 0, 0, tiled=True)  28.8 us
    ppermute x4, waiting for transfers between devices, padded_2(): lax.ppermute(head, axis, [((i + 1) % count, i) for i in range(ends)])  14.7 us
    mul x1, other arithmetic, block_gradient(): weighted = weight[None, :, None, None] * beam_gain * residual  11.7 us
    dot_general x2, matrix products, body(): jnp.dot(row_imag, packed, preferred_element_type=jnp.float32)  11.6 us
    convert_element_type x1, other arithmetic, block_gradient(): beam_gain = beam_block.astype(jnp.float32)[:, :, None, :]  11.3 us
    ppermute x4, starting transfers between devices, padded_2(): lax.ppermute(tail, axis, [(i, (i + 1) % count) for i in range(ends)])  11.2 us
  transfers between devices with their start and end apart: 9, of which 5 were waited for; matrix products, arithmetic and copies ran while one was open for 7% of the time, Pallas kernels for 0%

profile of v1, /device:TPU:13, one launch (start us, length us, event | category | flops | bytes accessed | tf_op | source)
XLA Modules:
  0.0 322.3 jit_solution(7335832101416945310)
XLA Ops:
  2.3 6.6 %all-to-all-start = ((bf16[16,32,4,256]{3,2,1,0:T(4,128)(2,1)}), bf16[16,32,4,256]{3,2,1,0:T(4,128)(2,1)S(1)}, u32[]{:S(2)}, u32[]{:S(2)}) async-start(bf16[16,32,4,256]{3,2,1,0:T(4,128)(2,1)} %broadcast_in_dim.14), calls=%async_computation | async-start | bytes 2097152 | tf_op jit(solution)/shard_map/all_to_all | solution.py:31
  8.9 11.3 %convert_element_type.111 = f32[512,32,256]{2,1,0:T(8,128)} convert(bf16[512,32,256]{2,1,0:T(8,128)(2,1)} %param.7) | non-fusion elementwise | flops 4194304 | bytes 25165824 | tf_op jit(solution)/shard_map/convert_element_type | solution.py:88
  21.4 11.7 %broadcast_multiply_fusion = f32[512,32,256]{2,1,0:T(8,128)} fusion(f32[32]{0:T(128)S(1)} %convert_multiply_fusion.1, bf16[512,32,256]{2,1,0:T(8,128)(2,1)} %param.7), kind=kLoop, calls=%fused_computation.16 | loop fusion | flops 8388608 | bytes 25165952 | tf_op jit(solution)/shard_map/mul | solution.py:91
  37.4 3.1 reshape.72
  43.2 6.6 %fusion.57 = f32[512,4,2,256]{3,0,2,1:T(8,128)S(1)} fusion(bf16[4,2,256,512]{3,2,1,0:T(8,128)(2,1)} %bitcast.93), kind=kOutput, calls=%fused_computation.66 | convolution fusion | flops 1078198272 | bytes 6291456 | tf_op jit(solution)/shard_map/dot_general | solution.py:142
  49.9 4.9 %fusion.63 = f32[512,4,2,256]{3,0,2,1:T(8,128)S(1)} fusion(bf16[4,2,256,512]{3,2,1,0:T(8,128)(2,1)S(1)} %bitcast.94), kind=kOutput, calls=%fused_computation.68 | convolution fusion | flops 1077936128 | bytes 6291456 | tf_op jit(solution)/shard_map/dot_general | solution.py:141
  56.4 23.7 %convert_bitcast_fusion.1 = bf16[512,4,2,256]{3,1,2,0:T(4,128)(2,1)} fusion(f32[512,32,256]{2,1,0:T(8,128)} %convert_element_type.111, f32[512,32,256]{2,1,0:T(8,128)} %broadcast_multiply_fusion, bf16[512,32,2,256]{3,2,1,0:T(2,128)(2,1)} %param.6, bf16[512,4,2,256]{3,0,2,1:T(8,128)(2,1)S(1)} %pad_maximum_fusion, f32[32,4]{0,1:T(4,128)S(1)} %copy-done.2), kind=kOutput, calls=%fused_computation.51 | convolution fusion | flops 176160896 | bytes 54526464 | tf_op jit(solution)/shard_map/cs,kczl->kszl/dot_general | solution.py:92
  80.1 3.4 %copy.31 = bf16[512,4,2,256]{0,3,2,1:T(8,128)(2,1)S(1)} copy(bf16[512,4,2,256]{3,1,2,0:T(4,128)(2,1)} %convert_bitcast_fusion.1) | data formatting | bytes 4194304 | tf_op jit(solution)/shard_map/convert_element_type | solution.py:93
  83.5 4.9 %fusion.33 = f32[512,4,2,256]{3,0,2,1:T(8,128)S(1)} fusion(bf16[512,4,2,256]{0,3,2,1:T(8,128)(2,1)S(1)} %copy.31), kind=kOutput, calls=%fused_computation.46 | convolution fusion | flops 1078198272 | bytes 6291456 | tf_op jit(solution)/shard_map/dot_general | solution.py:74
  88.4 4.9 %fusion.35 = f32[512,4,2,256]{3,0,2,1:T(8,128)S(1)} fusion(bf16[512,4,2,256]{0,3,2,1:T(8,128)(2,1)S(1)} %copy.31), kind=kOutput, calls=%fused_computation.48 | convolution fusion | flops 1077936128 | bytes 6291456 | tf_op jit(solution)/shard_map/dot_general | solution.py:73
  95.0 52.4 %all_to_all.20 = f32[16,32,4,256]{3,1,2,0:T(8,128)S(1)} all-to-all(f32[16,32,4,256]{3,1,2,0:T(8,128)S(1)} %fusion.31), channel_id=1, replica_groups=mesh['groups'=2,'chan'=16] {'chan'}, dimensions={0} | all-to-all | bytes 4194304 | tf_op jit(solution)/shard_map/all_to_all | solution.py:38
  148.4 3.6 %collective-permute-start = (f32[1,4,256]{2,0,1:T(1,128)S(1)}, f32[1,4,256]{2,0,1:T(1,128)S(1)}, u32[]{:S(2)}, u32[]{:S(2)}) collective-permute-start(f32[1,4,256]{2,0,1:T(1,128)S(1)} %get-tuple-element.25), channel_id=1, source_target_pairs={{0,1},{1,2},{2,3},{3,4},{4,5},{5,6},{6,7},{7,8},{8,9},{9,10},{10,1... | collective-permute-start | bytes 12296 | tf_op jit(solution)/shard_map/ppermute | solution.py:19
  154.0 3.9 %collective-permute-done.1 = f32[1,4,256]{2,0,1:T(1,128)S(1)} collective-permute-done((f32[1,4,256]{2,0,1:T(1,128)S(1)}, f32[1,4,256]{2,0,1:T(1,128)S(1)}, u32[]{:S(2)}, u32[]{:S(2)}) %collective-permute-start.1) | collective-permute-done | bytes 4128 | tf_op jit(solution)/shard_map/ppermute | solution.py:21
  162.4 3.4 %collective-permute-done.3 = f32[2,4,256]{2,0,1:T(2,128)S(1)} collective-permute-done((f32[2,4,256]{2,0,1:T(2,128)S(1)}, f32[2,4,256]{2,0,1:T(2,128)S(1)}, u32[]{:S(2)}, u32[]{:S(2)}) %collective-permute-start.3) | collective-permute-done | bytes 8224 | tf_op jit(solution)/shard_map/ppermute | solution.py:21
  166.6 28.8 %all_to_all.21 = bf16[16,32,4,256]{3,2,1,0:T(4,128)(2,1)S(1)} all-to-all(bf16[16,32,4,256]{3,2,1,0:T(4,128)(2,1)S(1)} %broadcast_in_dim.15), channel_id=1, replica_groups=mesh['groups'=2,'chan'=16] {'chan'}, dimensions={0} | all-to-all | bytes 2097152 | tf_op jit(solution)/shard_map/all_to_all | solution.py:31
  201.8 4.9 %fusion.54 = f32[512,4,2,256]{3,0,2,1:T(8,128)S(1)} fusion(bf16[4,2,256,512]{3,2,1,0:T(8,128)(2,1)S(1)} %bitcast.95), kind=kOutput, calls=%fused_computation.65 | convolution fusion | flops 1078198272 | bytes 6291456 | tf_op jit(solution)/shard_map/dot_general | solution.py:142
  206.7 4.9 %fusion.60 = f32[512,4,2,256]{3,0,2,1:T(8,128)S(1)} fusion(bf16[4,2,256,512]{3,2,1,0:T(8,128)(2,1)S(1)} %bitcast.96), kind=kOutput, calls=%fused_computation.67 | convolution fusion | flops 1077936128 | bytes 6291456 | tf_op jit(solution)/shard_map/dot_general | solution.py:141
  212.7 24.0 %convert_bitcast_fusion = bf16[512,4,2,256]{3,1,2,0:T(4,128)(2,1)} fusion(f32[512,32,256]{2,1,0:T(8,128)} %convert_element_type.111, f32[512,32,256]{2,1,0:T(8,128)} %broadcast_multiply_fusion, bf16[512,32,2,256]{3,2,1,0:T(2,128)(2,1)} %param.6, bf16[512,4,2,256]{3,0,2,1:T(8,128)(2,1)S(1)} %pad_maximum_fusion.1, f32[32,4]{0,1:T(4,128)S(1)} %copy-done.2), kind=kOutput, calls=%fused_computation.50 | convolution fusion | flops 176160896 | bytes 54526464 | tf_op jit(solution)/shard_map/cs,kczl->kszl/dot_general | solution.py:92
  239.7 4.9 %fusion.27 = f32[512,4,2,256]{3,0,2,1:T(8,128)S(1)} fusion(bf16[512,4,2,256]{0,3,2,1:T(8,128)(2,1)S(1)} %copy.38), kind=kOutput, calls=%fused_computation.40 | convolution fusion | flops 1078198272 | bytes 6291456 | tf_op jit(solution)/shard_map/dot_general | solution.py:74
  244.6 4.9 %fusion.29 = f32[512,4,2,256]{3,0,2,1:T(8,128)S(1)} fusion(bf16[512,4,2,256]{0,3,2,1:T(8,128)(2,1)S(1)} %copy.38), kind=kOutput, calls=%fused_computation.42 | convolution fusion | flops 1077936128 | bytes 6291456 | tf_op jit(solution)/shard_map/dot_general | solution.py:73
  251.1 52.1 %all_to_all.22 = f32[16,32,4,256]{3,1,2,0:T(8,128)S(1)} all-to-all(f32[16,32,4,256]{3,1,2,0:T(8,128)S(1)} %fusion.25), channel_id=1, replica_groups=mesh['groups'=2,'chan'=16] {'chan'}, dimensions={0} | all-to-all | bytes 4194304 | tf_op jit(solution)/shard_map/all_to_all | solution.py:38
  303.4 3.6 %collective-permute-start.4 = (f32[1,4,256]{2,0,1:T(1,128)S(1)}, f32[1,4,256]{2,0,1:T(1,128)S(1)}, u32[]{:S(2)}, u32[]{:S(2)}) collective-permute-start(f32[1,4,256]{2,0,1:T(1,128)S(1)} %get-tuple-element.21), channel_id=1, source_target_pairs={{0,1},{1,2},{2,3},{3,4},{4,5},{5,6},{6,7},{7,8},{8,9},{9,10},{10,1... | collective-permute-start | bytes 12296 | tf_op jit(solution)/shard_map/ppermute | solution.py:19
  309.0 3.9 %collective-permute-done.5 = f32[1,4,256]{2,0,1:T(1,128)S(1)} collective-permute-done((f32[1,4,256]{2,0,1:T(1,128)S(1)}, f32[1,4,256]{2,0,1:T(1,128)S(1)}, u32[]{:S(2)}, u32[]{:S(2)}) %collective-permute-start.5) | collective-permute-done | bytes 4128 | tf_op jit(solution)/shard_map/ppermute | solution.py:21
  317.4 3.5 %collective-permute-done.7 = f32[2,4,256]{2,0,1:T(2,128)S(1)} collective-permute-done((f32[2,4,256]{2,0,1:T(2,128)S(1)}, f32[2,4,256]{2,0,1:T(2,128)S(1)}, u32[]{:S(2)}, u32[]{:S(2)}) %collective-permute-start.7) | collective-permute-done | bytes 8224 | tf_op jit(solution)/shard_map/ppermute | solution.py:21
  (67 shorter events, 41.6 us)
Async XLA Ops:
  2.3 31.4 %all-to-all-start = ((bf16[16,32,4,256]{3,2,1,0:T(4,128)(2,1)}), bf16[16,32,4,256]{3,2,1,0:T(4,128)(2,1)S(1)}, u32[]{:S(2)}, u32[]{:S(2)}) async-start(bf16[16,32,4,256]{3,2,1,0:T(4,128)(2,1)} %broadcast_in_dim.14), calls=%async_computation | async-start | bytes 2097152 | tf_op jit(solution)/shard_map/all_to_all | solution.py:31
  8.9 12.4 %copy-start.6 = (s32[32]{0:T(128)S(1)}, s32[32]{0:T(128)}, u32[]{:S(2)}) copy-start(s32[32]{0:T(128)} %param.9) | copy-start | bytes 388
  43.2 6.7 %copy-start = (bf16[2048,512]{1,0:T(8,128)(2,1)S(1)}, bf16[2048,512]{1,0:T(8,128)(2,1)}, u32[]{:S(2)}) copy-start(bf16[2048,512]{1,0:T(8,128)(2,1)} %copy.48) | copy-start | bytes 6291460
  55.7 0.7 copy-start.2
  147.4 0.9 copy-start.1
  147.4 6.5 %copy-start.5 = (s32[4,2]{0,1:T(2,128)S(1)}, s32[4,2]{0,1:T(2,128)}, u32[]{:S(2)}) copy-start(s32[4,2]{0,1:T(2,128)} %param.10) | copy-start | bytes 100
  148.4 5.6 %collective-permute-start = (f32[1,4,256]{2,0,1:T(1,128)S(1)}, f32[1,4,256]{2,0,1:T(1,128)S(1)}, u32[]{:S(2)}, u32[]{:S(2)}) collective-permute-start(f32[1,4,256]{2,0,1:T(1,128)S(1)} %get-tuple-element.25), channel_id=1, source_target_pairs={{0,1},{1,2},{2,3},{3,4},{4,5},{5,6},{6,7},{7,8},{8,9},{9,10},{10,1... | collective-permute-start | bytes 12296 | tf_op jit(solution)/shard_map/ppermute | solution.py:19
  152.0 5.8 %collective-permute-start.1 = (f32[1,4,256]{2,0,1:T(1,128)S(1)}, f32[1,4,256]{2,0,1:T(1,128)S(1)}, u32[]{:S(2)}, u32[]{:S(2)}) collective-permute-start(f32[1,4,256]{2,0,1:T(1,128)S(1)} %get-tuple-element.26), channel_id=1, source_target_pairs={{1,0},{2,1},{3,2},{4,3},{5,4},{6,5},{7,6},{8,7},{9,8},{10,9},{11,1... | collective-permute-start | bytes 12296 | tf_op jit(solution)/shard_map/ppermute | solution.py:21
  158.0 4.4 %collective-permute-start.2 = (f32[2,4,256]{2,0,1:T(2,128)S(1)}, f32[2,4,256]{2,0,1:T(2,128)S(1)}, u32[]{:S(2)}, u32[]{:S(2)}) collective-permute-start(f32[2,4,256]{2,0,1:T(2,128)S(1)} %get-tuple-element.23), channel_id=1, source_target_pairs={{0,1},{1,2},{2,3},{3,4},{4,5},{5,6},{6,7},{7,8},{8,9},{9,10},{10,1... | collective-permute-start | bytes 24584 | tf_op jit(solution)/shard_map/ppermute | solution.py:19
  160.0 5.9 %collective-permute-start.3 = (f32[2,4,256]{2,0,1:T(2,128)S(1)}, f32[2,4,256]{2,0,1:T(2,128)S(1)}, u32[]{:S(2)}, u32[]{:S(2)}) collective-permute-start(f32[2,4,256]{2,0,1:T(2,128)S(1)} %get-tuple-element.24), channel_id=1, source_target_pairs={{1,0},{2,1},{3,2},{4,3},{5,4},{6,5},{7,6},{8,7},{9,8},{10,9},{11,1... | collective-permute-start | bytes 24584 | tf_op jit(solution)/shard_map/ppermute | solution.py:21
  162.4 3.7 %copy-start.3 = (f32[4]{0:T(128)}, f32[4]{0:T(128)S(1)}, u32[]{:S(2)}) copy-start(f32[4]{0:T(128)S(1)} %get-tuple-element.30) | copy-start | bytes 52
  303.2 17.7 %copy-start.4 = (f32[4]{0:T(128)S(1)}, f32[4]{0:T(128)}, u32[]{:S(2)}) copy-start(f32[4]{0:T(128)} %copy-done.3) | copy-start | bytes 52
  303.4 5.6 %collective-permute-start.4 = (f32[1,4,256]{2,0,1:T(1,128)S(1)}, f32[1,4,256]{2,0,1:T(1,128)S(1)}, u32[]{:S(2)}, u32[]{:S(2)}) collective-permute-start(f32[1,4,256]{2,0,1:T(1,128)S(1)} %get-tuple-element.21), channel_id=1, source_target_pairs={{0,1},{1,2},{2,3},{3,4},{4,5},{5,6},{6,7},{7,8},{8,9},{9,10},{10,1... | collective-permute-start | bytes 12296 | tf_op jit(solution)/shard_map/ppermute | solution.py:19
  307.1 5.8 %collective-permute-start.5 = (f32[1,4,256]{2,0,1:T(1,128)S(1)}, f32[1,4,256]{2,0,1:T(1,128)S(1)}, u32[]{:S(2)}, u32[]{:S(2)}) collective-permute-start(f32[1,4,256]{2,0,1:T(1,128)S(1)} %get-tuple-element.22), channel_id=1, source_target_pairs={{1,0},{2,1},{3,2},{4,3},{5,4},{6,5},{7,6},{8,7},{9,8},{10,9},{11,1... | collective-permute-start | bytes 12296 | tf_op jit(solution)/shard_map/ppermute | solution.py:21
  313.1 4.3 %collective-permute-start.6 = (f32[2,4,256]{2,0,1:T(2,128)S(1)}, f32[2,4,256]{2,0,1:T(2,128)S(1)}, u32[]{:S(2)}, u32[]{:S(2)}) collective-permute-start(f32[2,4,256]{2,0,1:T(2,128)S(1)} %get-tuple-element.19), channel_id=1, source_target_pairs={{0,1},{1,2},{2,3},{3,4},{4,5},{5,6},{6,7},{7,8},{8,9},{9,10},{10,1... | collective-permute-start | bytes 24584 | tf_op jit(solution)/shard_map/ppermute | solution.py:19
  315.0 5.9 %collective-permute-start.7 = (f32[2,4,256]{2,0,1:T(2,128)S(1)}, f32[2,4,256]{2,0,1:T(2,128)S(1)}, u32[]{:S(2)}, u32[]{:S(2)}) collective-permute-start(f32[2,4,256]{2,0,1:T(2,128)S(1)} %get-tuple-element.20), channel_id=1, source_target_pairs={{1,0},{2,1},{3,2},{4,3},{5,4},{6,5},{7,6},{8,7},{9,8},{10,9},{11,1... | collective-permute-start | bytes 24584 | tf_op jit(solution)/shard_map/ppermute | solution.py:21

commit v2 on v1

--- a/solution.py
+++ b/solution.py
@@ -27,16 +27,32 @@
 
 def gather_rows(strip, axis):
     count = lax.axis_size(axis)
-    copies = jnp.broadcast_to(strip[None], (count,) + strip.shape)
-    joined = lax.all_to_all(copies, axis, 0, 0, tiled=True)
+    bits = count.bit_length() - 1
+    assert 1 << bits == count
+    own = lax.axis_index(axis)
+    joined = strip
+    for depth, bit in enumerate(reversed(range(bits))):
+        partner = lax.ppermute(joined, axis, [(i, i ^ (1 << bit)) for i in range(count)])
+        upper = ((own >> bit) & 1) == 1
+        low = jnp.where(upper, partner, joined)
+        high = jnp.where(upper, joined, partner)
+        joined = jnp.stack([low, high], axis=depth)
     return joined.reshape((count * strip.shape[0],) + strip.shape[1:])
 
 
 def sum_rows(values, axis):
     count = lax.axis_size(axis)
-    chunks = values.reshape((count, values.shape[0] // count) + values.shape[1:])
-    received = lax.all_to_all(chunks, axis, 0, 0, tiled=True)
-    return received.sum(axis=0)
+    bits = count.bit_length() - 1
+    assert 1 << bits == count
+    own = lax.axis_index(axis)
+    split = values.reshape((2,) * bits + (values.shape[0] // count,) + values.shape[1:])
+    for bit in range(bits):
+        dim = bits - 1 - bit
+        side = (own >> bit) & 1
+        keep = lax.dynamic_index_in_dim(split, side, axis=dim, keepdims=False)
+        send = lax.dynamic_index_in_dim(split, 1 - side, axis=dim, keepdims=False)
+        split = keep + lax.ppermute(send, axis, [(i, i ^ (1 << bit)) for i in range(count)])
+    return split
 
 
 def dft_tables(length):

time: 329 us -> 419 us (1.27)
  the two profiles are of different devices: /device:TPU:13 before, /device:TPU:1 now
where the time goes in v2:
time: 419 us; the launch traced here: 412 us
  other arithmetic  168 us (40%)
  matrix products  87.9 us (21%)
  waiting for transfers between devices  86.9 us (21%)
  starting transfers between devices  48.7 us (12%)
  local copies, waits for them, and re-layouts  19.6 us (5%)
    mul x3, other arithmetic, block_gradient(): weighted = weight[None, :, None, None] * beam_gain * residual  140 us
    ppermute x8, waiting for transfers between devices, sum_rows(): lax.ppermute(send, axis, [(i, i ^ 1 << bit) for i in range(count)])  53.3 us
    dot_general x2, matrix products, block_gradient(): predicted = jnp.einsum('ct,ktzl->kczl', mix_block, fourier)  27.1 us
    ppermute x8, waiting for transfers between devices, gather_rows(): lax.ppermute(joined, axis, [(i, i ^ 1 << bit) for i in range(count)])  22.5 us
    dot_general x2, matrix products, block_gradient(): summed = jnp.einsum('cs,kczl->kszl', mix_block, weighted)  18.8 us
    ppermute x8, starting transfers between devices, gather_rows(): lax.ppermute(joined, axis, [(i, i ^ 1 << bit) for i in range(count)])  17.4 us
    ppermute x4, starting transfers between devices, padded_2(): lax.ppermute(tail, axis, [(i, (i + 1) % count) for i in range(ends)])  13.4 us
    convert_element_type x1, other arithmetic, block_gradient(): beam_gain = beam_block.astype(jnp.float32)[:, :, None, :]  11.3 us
  transfers between devices with their start and end apart: 24, of which 19 were waited for; matrix products, arithmetic and copies ran while one was open for 6% of the time, Pallas kernels for 0%

profile of v2, /device:TPU:1, one launch (start us, length us, event | category | flops | bytes accessed | tf_op | source)
XLA Modules:
  0.0 411.6 jit_solution(15290321304813867996)
XLA Ops:
  22.4 11.7 %broadcast_multiply_fusion = f32[512,32,256]{2,1,0:T(8,128)} fusion(f32[32]{0:T(128)S(1)} %convert_multiply_fusion.1, bf16[512,32,256]{2,1,0:T(8,128)(2,1)} %param.7), kind=kLoop, calls=%fused_computation.10 | loop fusion | flops 8388608 | bytes 25165952 | tf_op jit(solution)/shard_map/mul | solution.py:107
  34.1 11.3 %convert_element_type.108 = f32[512,32,256]{2,1,0:T(8,128)} convert(bf16[512,32,256]{2,1,0:T(8,128)(2,1)} %param.7) | non-fusion elementwise | flops 4194304 | bytes 25165824 | tf_op jit(solution)/shard_map/convert_element_type | solution.py:104
  55.0 4.9 %fusion.42 = f32[512,4,2,256]{3,0,2,1:T(8,128)S(1)} fusion(bf16[4,2,256,512]{3,2,1,0:T(8,128)(2,1)S(1)} %bitcast.193), kind=kOutput, calls=%fused_computation.77 | convolution fusion | flops 1078198272 | bytes 6291456 | tf_op jit(solution)/shard_map/dot_general | solution.py:158
  59.9 4.9 %fusion.48 = f32[512,4,2,256]{3,0,2,1:T(8,128)S(1)} fusion(bf16[4,2,256,512]{3,2,1,0:T(8,128)(2,1)S(1)} %bitcast.194), kind=kOutput, calls=%fused_computation.79 | convolution fusion | flops 1077936128 | bytes 6291456 | tf_op jit(solution)/shard_map/dot_general | solution.py:157
  65.9 13.7 %fusion.8 = f32[512,2,256,32]{2,3,1,0:T(8,128)} fusion(bf16[512,4,2,256]{3,0,2,1:T(8,128)(2,1)S(1)} %pad_maximum_fusion, f32[32,4]{0,1:T(4,128)S(1)} %copy-done), kind=kOutput, calls=%fused_computation.15 | convolution fusion | flops 67108864 | bytes 35652096 | tf_op jit(solution)/shard_map/ct,ktzl->kczl/dot_general | solution.py:103
  79.6 64.0 %fusion = bf16[512,32,2,256]{3,2,1,0:T(2,128)(2,1)} fusion(bf16[512,32,2,256]{3,2,1,0:T(2,128)(2,1)} %param.6, f32[512,2,256,32]{2,3,1,0:T(8,128)} %fusion.8, f32[512,32,256]{2,1,0:T(8,128)} %convert_element_type.108, f32[512,32,256]{2,1,0:T(8,128)} %broadcast_multiply_fusion), kind=kLoop, calls=%fused_computation.2 | loop fusion | flops 41943040 | bytes 100663296 | tf_op jit(solution)/shard_map/mul | solution.py:107
  143.6 9.4 %convert_bitcast_fusion.1 = bf16[512,4,2,256]{3,1,2,0:T(4,128)(2,1)} fusion(bf16[512,32,2,256]{3,2,1,0:T(2,128)(2,1)} %fusion, f32[32,4]{0,1:T(4,128)S(1)} %copy-done), kind=kOutput, calls=%fused_computation.46 | convolution fusion | flops 67108864 | bytes 18874880 | tf_op jit(solution)/shard_map/cs,kczl->kszl/dot_general | solution.py:108
  156.1 4.9 %fusion.22 = f32[512,4,2,256]{3,0,2,1:T(8,128)S(1)} fusion(bf16[512,4,2,256]{0,3,2,1:T(8,128)(2,1)S(1)} %copy.18), kind=kOutput, calls=%fused_computation.41 | convolution fusion | flops 1078198272 | bytes 6291456 | tf_op jit(solution)/shard_map/dot_general | solution.py:90
  161.0 4.9 %fusion.24 = f32[512,4,2,256]{3,0,2,1:T(8,128)S(1)} fusion(bf16[512,4,2,256]{0,3,2,1:T(8,128)(2,1)S(1)} %copy.18), kind=kOutput, calls=%fused_computation.43 | convolution fusion | flops 1077936128 | bytes 6291456 | tf_op jit(solution)/shard_map/dot_general | solution.py:89
  173.6 11.9 %collective-permute-done.5 = f32[2,2,32,4,256]{4,2,3,1,0:T(8,128)S(1)} collective-permute-done((f32[2,2,32,4,256]{4,2,3,1,0:T(8,128)S(1)}, f32[2,2,32,4,256]{4,2,3,1,0:T(8,128)S(1)}, u32[]{:S(2)}, u32[]{:S(2)}) %collective-permute-start.5) | collective-permute-done | bytes 524320 | tf_op jit(solution)/shard_map/ppermute | solution.py:54
  186.2 6.4 %collective-permute-done.6 = f32[2,32,4,256]{3,1,2,0:T(8,128)S(1)} collective-permute-done((f32[2,32,4,256]{3,1,2,0:T(8,128)S(1)}, f32[2,32,4,256]{3,1,2,0:T(8,128)S(1)}, u32[]{:S(2)}, u32[]{:S(2)}) %collective-permute-start.6) | collective-permute-done | bytes 262176 | tf_op jit(solution)/shard_map/ppermute | solution.py:54
  195.7 5.8 %collective-permute-done.7 = f32[32,4,256]{2,1,0:T(4,128)S(1)} collective-permute-done((f32[32,4,256]{2,1,0:T(4,128)S(1)}, f32[32,4,256]{2,1,0:T(4,128)S(1)}, u32[]{:S(2)}, u32[]{:S(2)}) %collective-permute-start.7) | collective-permute-done | bytes 131104 | tf_op jit(solution)/shard_map/ppermute | solution.py:54
  231.6 5.9 %collective-permute-done.14 = bf16[2,2,32,4,256]{4,3,2,0,1:T(4,128)(2,1)S(1)} collective-permute-done((bf16[2,2,32,4,256]{4,3,2,0,1:T(4,128)(2,1)S(1)}, bf16[2,2,32,4,256]{4,3,2,0,1:T(4,128)(2,1)S(1)}, u32[]{:S(2)}, u32[]{:S(2)}) %collective-permute-start.14) | collective-permute-done | bytes 262176 | tf_op jit(solution)/shard_map/ppermute | solution.py:35
  249.8 4.9 %fusion.39 = f32[512,4,2,256]{3,0,2,1:T(8,128)S(1)} fusion(bf16[4,2,256,512]{3,2,1,0:T(8,128)(2,1)S(1)} %bitcast.195), kind=kOutput, calls=%fused_computation.76 | convolution fusion | flops 1078198272 | bytes 6291456 | tf_op jit(solution)/shard_map/dot_general | solution.py:158
  254.7 4.9 %fusion.45 = f32[512,4,2,256]{3,0,2,1:T(8,128)S(1)} fusion(bf16[4,2,256,512]{3,2,1,0:T(8,128)(2,1)S(1)} %bitcast.196), kind=kOutput, calls=%fused_computation.78 | convolution fusion | flops 1077936128 | bytes 6291456 | tf_op jit(solution)/shard_map/dot_general | solution.py:157
  260.7 13.4 %fusion.6 = f32[512,2,256,32]{2,3,1,0:T(8,128)} fusion(bf16[512,4,2,256]{3,0,2,1:T(8,128)(2,1)S(1)} %pad_maximum_fusion.1, f32[32,4]{0,1:T(4,128)S(1)} %copy-done), kind=kOutput, calls=%fused_computation.13 | convolution fusion | flops 67108864 | bytes 35652096 | tf_op jit(solution)/shard_map/ct,ktzl->kczl/dot_general | solution.py:103
  274.1 64.0 %fusion.1 = bf16[512,32,2,256]{3,2,1,0:T(2,128)(2,1)} fusion(bf16[512,32,2,256]{3,2,1,0:T(2,128)(2,1)} %param.6, f32[512,2,256,32]{2,3,1,0:T(8,128)} %fusion.6, f32[512,32,256]{2,1,0:T(8,128)} %convert_element_type.108, f32[512,32,256]{2,1,0:T(8,128)} %broadcast_multiply_fusion), kind=kLoop, calls=%fused_computation.3 | loop fusion | flops 41943040 | bytes 100663296 | tf_op jit(solution)/shard_map/mul | solution.py:107
  338.1 9.4 %convert_bitcast_fusion = bf16[512,4,2,256]{3,1,2,0:T(4,128)(2,1)} fusion(bf16[512,32,2,256]{3,2,1,0:T(2,128)(2,1)} %fusion.1, f32[32,4]{0,1:T(4,128)S(1)} %copy-done), kind=kOutput, calls=%fused_computation.45 | convolution fusion | flops 67108864 | bytes 18874880 | tf_op jit(solution)/shard_map/cs,kczl->kszl/dot_general | solution.py:108
  350.5 4.9 %fusion.16 = f32[512,4,2,256]{3,0,2,1:T(8,128)S(1)} fusion(bf16[512,4,2,256]{0,3,2,1:T(8,128)(2,1)S(1)} %copy.26), kind=kOutput, calls=%fused_computation.35 | convolution fusion | flops 1078198272 | bytes 6291456 | tf_op jit(solution)/shard_map/dot_general | solution.py:90
  355.4 4.9 %fusion.18 = f32[512,4,2,256]{3,0,2,1:T(8,128)S(1)} fusion(bf16[512,4,2,256]{0,3,2,1:T(8,128)(2,1)S(1)} %copy.26), kind=kOutput, calls=%fused_computation.37 | convolution fusion | flops 1077936128 | bytes 6291456 | tf_op jit(solution)/shard_map/dot_general | solution.py:89
  366.5 11.7 %collective-permute-done.17 = f32[2,2,32,4,256]{4,2,3,1,0:T(8,128)S(1)} collective-permute-done((f32[2,2,32,4,256]{4,2,3,1,0:T(8,128)S(1)}, f32[2,2,32,4,256]{4,2,3,1,0:T(8,128)S(1)}, u32[]{:S(2)}, u32[]{:S(2)}) %collective-permute-start.17) | collective-permute-done | bytes 524320 | tf_op jit(solution)/shard_map/ppermute | solution.py:54
  378.6 6.4 %collective-permute-done.18 = f32[2,32,4,256]{3,1,2,0:T(8,128)S(1)} collective-permute-done((f32[2,32,4,256]{3,1,2,0:T(8,128)S(1)}, f32[2,32,4,256]{3,1,2,0:T(8,128)S(1)}, u32[]{:S(2)}, u32[]{:S(2)}) %collective-permute-start.18) | collective-permute-done | bytes 262176 | tf_op jit(solution)/shard_map/ppermute | solution.py:54
  387.0 6.0 %collective-permute-done.19 = f32[32,4,256]{2,1,0:T(4,128)S(1)} collective-permute-done((f32[32,4,256]{2,1,0:T(4,128)S(1)}, f32[32,4,256]{2,1,0:T(4,128)S(1)}, u32[]{:S(2)}, u32[]{:S(2)}) %collective-permute-start.19) | collective-permute-done | bytes 131104 | tf_op jit(solution)/shard_map/ppermute | solution.py:54
  393.2 5.0 %collective-permute-start.20 = (f32[1,4,256]{2,1,0:T(4,128)S(1)}, f32[1,4,256]{2,1,0:T(4,128)S(1)}, u32[]{:S(2)}, u32[]{:S(2)}) collective-permute-start(f32[1,4,256]{2,1,0:T(4,128)S(1)} %get-tuple-element.37), channel_id=1, source_target_pairs={{0,1},{1,2},{2,3},{3,4},{4,5},{5,6},{6,7},{7,8},{8,9},{9,10},{10,1... | collective-permute-start | bytes 12296 | tf_op jit(solution)/shard_map/ppermute | solution.py:19
  (121 shorter events, 115.6 us)
Async XLA Ops:
  0.9 4.9 %collective-permute-start = (bf16[32,4,256]{2,1,0:T(4,128)(2,1)S(1)}, bf16[32,4,256]{2,1,0:T(4,128)(2,1)S(1)}, u32[]{:S(2)}, u32[]{:S(2)}) collective-permute-start(bf16[32,4,256]{2,1,0:T(4,128)(2,1)S(1)} %convert_element_type.110), channel_id=1, source_target_pairs={{0,8},{1,9},{2,10},{3,11},{4,12},{5,13},{6,14},{7,15},{8,0},{9,1},... | collective-permute-start | bytes 196616 | tf_op jit(solution)/shard_map/ppermute | solution.py:35
  6.9 4.7 %collective-permute-start.1 = (bf16[2,32,4,256]{3,2,1,0:T(4,128)(2,1)S(1)}, bf16[2,32,4,256]{3,2,1,0:T(4,128)(2,1)S(1)}, u32[]{:S(2)}, u32[]{:S(2)}) collective-permute-start(bf16[2,32,4,256]{3,2,1,0:T(4,128)(2,1)S(1)} %pad_maximum_fusion.21), channel_id=1, source_target_pairs={{0,4},{1,5},{2,6},{3,7},{4,0},{5,1},{6,2},{7,3},{8,12},{9,13},{10,... | collective-permute-start | bytes 393224 | tf_op jit(solution)/shard_map/ppermute | solution.py:35
  11.9 5.3 %collective-permute-start.2 = (bf16[2,2,32,4,256]{4,3,2,0,1:T(4,128)(2,1)S(1)}, bf16[2,2,32,4,256]{4,3,2,0,1:T(4,128)(2,1)S(1)}, u32[]{:S(2)}, u32[]{:S(2)}) collective-permute-start(bf16[2,2,32,4,256]{4,3,2,0,1:T(4,128)(2,1)S(1)} %pad_maximum_fusion.8), channel_id=1, source_target_pairs={{0,2},{1,3},{2,0},{3,1},{4,6},{5,7},{6,4},{7,5},{8,10},{9,11},{10,... | collective-permute-start | bytes 786440 | tf_op jit(solution)/shard_map/ppermute | solution.py:35
  17.9 28.6 %collective-permute-start.3 = (bf16[2,2,2,32,4,256]{5,4,3,0,1,2:T(4,128)(2,1)S(1)}, bf16[2,2,2,32,4,256]{5,4,3,0,1,2:T(4,128)(2,1)S(1)}, u32[]{:S(2)}, u32[]{:S(2)}) collective-permute-start(bf16[2,2,2,32,4,256]{5,4,3,0,1,2:T(4,128)(2,1)S(1)} %pad_maximum_fusion.6), channel_id=1, source_target_pairs={{0,1},{1,0},{2,3},{3,2},{4,5},{5,4},{6,7},{7,6},{8,9},{9,8},{10,11... | collective-permute-start | bytes 1572872 | tf_op jit(solution)/shard_map/ppermute | solution.py:35
  167.7 2.9 collective-permute-start.4
  172.1 13.4 %collective-permute-start.5 = (f32[2,2,32,4,256]{4,2,3,1,0:T(8,128)S(1)}, f32[2,2,32,4,256]{4,2,3,1,0:T(8,128)S(1)}, u32[]{:S(2)}, u32[]{:S(2)}) collective-permute-start(f32[2,2,32,4,256]{4,2,3,1,0:T(8,128)S(1)} %dynamic-slice_bitcast_fusion.3), channel_id=1, source_target_pairs={{0,2},{1,3},{2,0},{3,1},{4,6},{5,7},{6,4},{7,5},{8,10},{9,11},{10,... | collective-permute-start | bytes 1572872 | tf_op jit(solution)/shard_map/ppermute | solution.py:54
  185.6 6.9 %collective-permute-start.6 = (f32[2,32,4,256]{3,1,2,0:T(8,128)S(1)}, f32[2,32,4,256]{3,1,2,0:T(8,128)S(1)}, u32[]{:S(2)}, u32[]{:S(2)}) collective-permute-start(f32[2,32,4,256]{3,1,2,0:T(8,128)S(1)} %dynamic-slice_bitcast_fusion.5), channel_id=1, source_target_pairs={{0,4},{1,5},{2,6},{3,7},{4,0},{5,1},{6,2},{7,3},{8,12},{9,13},{10,... | collective-permute-start | bytes 786440 | tf_op jit(solution)/shard_map/ppermute | solution.py:54
  192.7 8.8 %collective-permute-start.7 = (f32[32,4,256]{2,1,0:T(4,128)S(1)}, f32[32,4,256]{2,1,0:T(4,128)S(1)}, u32[]{:S(2)}, u32[]{:S(2)}) collective-permute-start(f32[32,4,256]{2,1,0:T(4,128)S(1)} %bitcast.201), channel_id=1, source_target_pairs={{0,8},{1,9},{2,10},{3,11},{4,12},{5,13},{6,14},{7,15},{8,0},{9,1},... | collective-permute-start | bytes 393224 | tf_op jit(solution)/shard_map/ppermute | solution.py:54
  201.6 6.5 %collective-permute-start.8 = (f32[1,4,256]{2,1,0:T(4,128)S(1)}, f32[1,4,256]{2,1,0:T(4,128)S(1)}, u32[]{:S(2)}, u32[]{:S(2)}) collective-permute-start(f32[1,4,256]{2,1,0:T(4,128)S(1)} %get-tuple-element.43), channel_id=1, source_target_pairs={{0,1},{1,2},{2,3},{3,4},{4,5},{5,6},{6,7},{7,8},{8,9},{9,10},{10,1... | collective-permute-start | bytes 12296 | tf_op jit(solution)/shard_map/ppermute | solution.py:19
  206.2 4.9 %collective-permute-start.9 = (f32[1,4,256]{2,1,0:T(4,128)S(1)}, f32[1,4,256]{2,1,0:T(4,128)S(1)}, u32[]{:S(2)}, u32[]{:S(2)}) collective-permute-start(f32[1,4,256]{2,1,0:T(4,128)S(1)} %get-tuple-element.44), channel_id=1, source_target_pairs={{1,0},{2,1},{3,2},{4,3},{5,4},{6,5},{7,6},{8,7},{9,8},{10,9},{11,1... | collective-permute-start | bytes 12296 | tf_op jit(solution)/shard_map/ppermute | solution.py:21
  211.4 4.4 %collective-permute-start.10 = (f32[2,4,256]{2,1,0:T(4,128)S(1)}, f32[2,4,256]{2,1,0:T(4,128)S(1)}, u32[]{:S(2)}, u32[]{:S(2)}) collective-permute-start(f32[2,4,256]{2,1,0:T(4,128)S(1)} %get-tuple-element.41), channel_id=1, source_target_pairs={{0,1},{1,2},{2,3},{3,4},{4,5},{5,6},{6,7},{7,8},{8,9},{9,10},{10,1... | collective-permute-start | bytes 24584 | tf_op jit(solution)/shard_map/ppermute | solution.py:19
  213.3 5.0 %collective-permute-start.11 = (f32[2,4,256]{2,1,0:T(4,128)S(1)}, f32[2,4,256]{2,1,0:T(4,128)S(1)}, u32[]{:S(2)}, u32[]{:S(2)}) collective-permute-start(f32[2,4,256]{2,1,0:T(4,128)S(1)} %get-tuple-element.42), channel_id=1, source_target_pairs={{1,0},{2,1},{3,2},{4,3},{5,4},{6,5},{7,6},{8,7},{9,8},{10,9},{11,1... | collective-permute-start | bytes 24584 | tf_op jit(solution)/shard_map/ppermute | solution.py:21
  218.6 6.1 %collective-permute-start.12 = (bf16[32,4,256]{2,1,0:T(4,128)(2,1)S(1)}, bf16[32,4,256]{2,1,0:T(4,128)(2,1)S(1)}, u32[]{:S(2)}, u32[]{:S(2)}) collective-permute-start(bf16[32,4,256]{2,1,0:T(4,128)(2,1)S(1)} %get-tuple-element.7), channel_id=1, source_target_pairs={{0,8},{1,9},{2,10},{3,11},{4,12},{5,13},{6,14},{7,15},{8,0},{9,1},... | collective-permute-start | bytes 196616 | tf_op jit(solution)/shard_map/ppermute | solution.py:35
  224.9 4.7 %collective-permute-start.13 = (bf16[2,32,4,256]{3,2,1,0:T(4,128)(2,1)S(1)}, bf16[2,32,4,256]{3,2,1,0:T(4,128)(2,1)S(1)}, u32[]{:S(2)}, u32[]{:S(2)}) collective-permute-start(bf16[2,32,4,256]{3,2,1,0:T(4,128)(2,1)S(1)} %pad_maximum_fusion.22), channel_id=1, source_target_pairs={{0,4},{1,5},{2,6},{3,7},{4,0},{5,1},{6,2},{7,3},{8,12},{9,13},{10,... | collective-permute-start | bytes 393224 | tf_op jit(solution)/shard_map/ppermute | solution.py:35
  230.0 7.5 %collective-permute-start.14 = (bf16[2,2,32,4,256]{4,3,2,0,1:T(4,128)(2,1)S(1)}, bf16[2,2,32,4,256]{4,3,2,0,1:T(4,128)(2,1)S(1)}, u32[]{:S(2)}, u32[]{:S(2)}) collective-permute-start(bf16[2,2,32,4,256]{4,3,2,0,1:T(4,128)(2,1)S(1)} %pad_maximum_fusion.10), channel_id=1, source_target_pairs={{0,2},{1,3},{2,0},{3,1},{4,6},{5,7},{6,4},{7,5},{8,10},{9,11},{10,... | collective-permute-start | bytes 786440 | tf_op jit(solution)/shard_map/ppermute | solution.py:35
  238.2 2.9 collective-permute-start.15
  362.1 2.7 collective-permute-start.16
  365.0 13.2 %collective-permute-start.17 = (f32[2,2,32,4,256]{4,2,3,1,0:T(8,128)S(1)}, f32[2,2,32,4,256]{4,2,3,1,0:T(8,128)S(1)}, u32[]{:S(2)}, u32[]{:S(2)}) collective-permute-start(f32[2,2,32,4,256]{4,2,3,1,0:T(8,128)S(1)} %dynamic-slice_bitcast_fusion.2), channel_id=1, source_target_pairs={{0,2},{1,3},{2,0},{3,1},{4,6},{5,7},{6,4},{7,5},{8,10},{9,11},{10,... | collective-permute-start | bytes 1572872 | tf_op jit(solution)/shard_map/ppermute | solution.py:54
  378.3 6.7 %collective-permute-start.18 = (f32[2,32,4,256]{3,1,2,0:T(8,128)S(1)}, f32[2,32,4,256]{3,1,2,0:T(8,128)S(1)}, u32[]{:S(2)}, u32[]{:S(2)}) collective-permute-start(f32[2,32,4,256]{3,1,2,0:T(8,128)S(1)} %dynamic-slice_bitcast_fusion.4), channel_id=1, source_target_pairs={{0,4},{1,5},{2,6},{3,7},{4,0},{5,1},{6,2},{7,3},{8,12},{9,13},{10,... | collective-permute-start | bytes 786440 | tf_op jit(solution)/shard_map/ppermute | solution.py:54
  385.2 7.9 %collective-permute-start.19 = (f32[32,4,256]{2,1,0:T(4,128)S(1)}, f32[32,4,256]{2,1,0:T(4,128)S(1)}, u32[]{:S(2)}, u32[]{:S(2)}) collective-permute-start(f32[32,4,256]{2,1,0:T(4,128)S(1)} %bitcast.202), channel_id=1, source_target_pairs={{0,8},{1,9},{2,10},{3,11},{4,12},{5,13},{6,14},{7,15},{8,0},{9,1},... | collective-permute-start | bytes 393224 | tf_op jit(solution)/shard_map/ppermute | solution.py:54
  393.2 7.0 %collective-permute-start.20 = (f32[1,4,256]{2,1,0:T(4,128)S(1)}, f32[1,4,256]{2,1,0:T(4,128)S(1)}, u32[]{:S(2)}, u32[]{:S(2)}) collective-permute-start(f32[1,4,256]{2,1,0:T(4,128)S(1)} %get-tuple-element.37), channel_id=1, source_target_pairs={{0,1},{1,2},{2,3},{3,4},{4,5},{5,6},{6,7},{7,8},{8,9},{9,10},{10,1... | collective-permute-start | bytes 12296 | tf_op jit(solution)/shard_map/ppermute | solution.py:19
  398.2 4.9 %collective-permute-start.21 = (f32[1,4,256]{2,1,0:T(4,128)S(1)}, f32[1,4,256]{2,1,0:T(4,128)S(1)}, u32[]{:S(2)}, u32[]{:S(2)}) collective-permute-start(f32[1,4,256]{2,1,0:T(4,128)S(1)} %get-tuple-element.38), channel_id=1, source_target_pairs={{1,0},{2,1},{3,2},{4,3},{5,4},{6,5},{7,6},{8,7},{9,8},{10,9},{11,1... | collective-permute-start | bytes 12296 | tf_op jit(solution)/shard_map/ppermute | solution.py:21
  403.4 4.3 %collective-permute-start.22 = (f32[2,4,256]{2,1,0:T(4,128)S(1)}, f32[2,4,256]{2,1,0:T(4,128)S(1)}, u32[]{:S(2)}, u32[]{:S(2)}) collective-permute-start(f32[2,4,256]{2,1,0:T(4,128)S(1)} %get-tuple-element.35), channel_id=1, source_target_pairs={{0,1},{1,2},{2,3},{3,4},{4,5},{5,6},{6,7},{7,8},{8,9},{9,10},{10,1... | collective-permute-start | bytes 24584 | tf_op jit(solution)/shard_map/ppermute | solution.py:19
  405.4 5.0 %collective-permute-start.23 = (f32[2,4,256]{2,1,0:T(4,128)S(1)}, f32[2,4,256]{2,1,0:T(4,128)S(1)}, u32[]{:S(2)}, u32[]{:S(2)}) collective-permute-start(f32[2,4,256]{2,1,0:T(4,128)S(1)} %get-tuple-element.36), channel_id=1, source_target_pairs={{1,0},{2,1},{3,2},{4,3},{5,4},{6,5},{7,6},{8,7},{9,8},{10,9},{11,1... | collective-permute-start | bytes 24584 | tf_op jit(solution)/shard_map/ppermute | solution.py:21
  (5 other events, 176.1 us)
